TPU v7x, 256 devices: a whole 4x4x8 slice. The times are simulated.
256 devices in a mesh: expert: 16 (over z, core), fsdp: 16 (over x, y).
Axes of the slice: x: 4, y: 4, z: 8, core: 2. Of those that a mesh axis runs over, the one named last changes fastest.
Arguments:
- tokens: bfloat16 [32768, 2048], P(('expert', 'fsdp')), may hold values from -6 to 6
- expert_ids: int32 [32768, 4], P(('expert', 'fsdp')), may hold values from 0 to 15, all different within a row; in each aligned block of 128 rows (0 to 127, 128 to 255, ...) at most 36 rows name the same one
- route_probs: float32 [32768, 4], P(('expert', 'fsdp')), may hold values from 0.1 to 1
- gate_weight: bfloat16 [16, 2048, 704], P('expert', 'fsdp'), may hold values from -0.125 to 0.125
- up_weight: bfloat16 [16, 2048, 704], P('expert', 'fsdp'), may hold values from -0.125 to 0.125
- down_weight: bfloat16 [16, 704, 2048], P('expert', None, 'fsdp'), may hold values from -0.21875 to 0.21875
- cotangent: bfloat16 [32768, 2048], P(('expert', 'fsdp')), may hold values from -0.59765625 to 0.59765625
Outputs:
- mixed: bfloat16 [32768, 2048], P(('expert', 'fsdp'))
- grad_probs: float32 [32768, 4], P(('expert', 'fsdp'))
- grad_tokens: bfloat16 [32768, 2048], P(('expert', 'fsdp'))
- grad_gate: bfloat16 [16, 2048, 704], P('expert', 'fsdp')
- grad_up: bfloat16 [16, 2048, 704], P('expert', 'fsdp')
- grad_down: bfloat16 [16, 704, 2048], P('expert', None, 'fsdp')
Inputs may be any that keep to these rules, and one draw needn't show every extreme that they name: `expert_ids`: each token names 4 different experts; among the 128 tokens of one device no expert is named more than 36 times.
All inputs are finite; a program needn't handle non-finite values.
Results may differ from a plain program's by a relative error of at most 0.014.
Values may be sent and summed in bfloat16 or wider, within the bound.
No kernel may reach another device: no remote copies, remote signals or barrier semaphores. Data moves between devices by JAX's collectives and lax.ppermute only.
A program may use at most 128 MiB of HBM per device.

v0:
```python
import jax
import jax.numpy as jnp
from jax import lax
from jax.sharding import PartitionSpec as P


def routing(id_rows, experts, capacity):
    flat_ids = id_rows.reshape(-1)
    onehot = (flat_ids[:, None] == jnp.arange(experts, dtype=jnp.int32)[None, :]).astype(jnp.int32)
    before = jnp.cumsum(onehot, axis=0) - onehot
    slot_index = jnp.sum(before * onehot, axis=1)
    target = flat_ids * capacity + slot_index
    slots = experts * capacity
    dispatch = jnp.arange(slots, dtype=jnp.int32)[:, None] == target[None, :]
    return (dispatch, jnp.sum(onehot, axis=0))


def expert_forward(routed, live_mask, w_gate, w_up, w_down_blocks):
    gate_pre = jnp.dot(routed, w_gate, preferred_element_type=jnp.float32)
    up_pre = jnp.dot(routed, w_up, preferred_element_type=jnp.float32)
    hidden = (jax.nn.silu(gate_pre) * up_pre * live_mask[:, None]).astype(jnp.bfloat16)
    expert_out = jnp.einsum(
        "sf,jfd->sjd", hidden, w_down_blocks, preferred_element_type=jnp.float32
    ).astype(jnp.bfloat16)
    return (gate_pre, up_pre, hidden, expert_out.reshape(hidden.shape[0], -1))


def expert_backward(routed, grad_rows, gate_pre, up_pre, hidden, w_gate, w_up, w_down_blocks):
    grad_blocks = grad_rows.reshape(grad_rows.shape[0], w_down_blocks.shape[0], -1)
    grad_hidden = jnp.einsum(
        "sjd,jfd->sf", grad_blocks, w_down_blocks, preferred_element_type=jnp.float32
    )
    logistic = jax.nn.sigmoid(gate_pre)
    activated = gate_pre * logistic
    slope = logistic * (1.0 + gate_pre * (1.0 - logistic))
    grad_gate_pre = (grad_hidden * up_pre * slope).astype(jnp.bfloat16)
    grad_up_pre = (grad_hidden * activated).astype(jnp.bfloat16)
    row_grad = (
        jnp.dot(grad_gate_pre, w_gate.T, preferred_element_type=jnp.float32)
        + jnp.dot(grad_up_pre, w_up.T, preferred_element_type=jnp.float32)
    ).astype(jnp.bfloat16)
    term_gate = jnp.dot(routed.T, grad_gate_pre, preferred_element_type=jnp.float32)
    term_up = jnp.dot(routed.T, grad_up_pre, preferred_element_type=jnp.float32)
    term_down_t = jnp.dot(grad_rows.T, hidden, preferred_element_type=jnp.float32)
    return (row_grad, term_gate, term_up, term_down_t)


def gather_fsdp(shard, n_fsdp):
    copies = jnp.broadcast_to(shard[None], (n_fsdp,) + shard.shape)
    return lax.all_to_all(copies, "fsdp", split_axis=0, concat_axis=0, tiled=True)


def scatter_sum_fsdp(terms, n_fsdp):
    stacked = jnp.stack([t.astype(jnp.bfloat16) for t in terms], axis=0)
    count, rows = (stacked.shape[0], stacked.shape[1] // n_fsdp)
    blocks = stacked.reshape((count, n_fsdp, rows) + stacked.shape[2:]).swapaxes(0, 1)
    got = lax.all_to_all(blocks, "fsdp", split_axis=0, concat_axis=0, tiled=True)
    summed = jnp.sum(got.astype(jnp.float32), axis=0).astype(jnp.bfloat16)
    return [summed[i] for i in range(count)]


def per_device(tokens, expert_ids, route_probs, gate_weight, up_weight, down_weight, cotangent):
    n_expert = lax.axis_size("expert")
    n_fsdp = lax.axis_size("fsdp")
    experts = n_expert * gate_weight.shape[0]
    tok_dev, choose = expert_ids.shape
    features = tokens.shape[1]
    capacity = tok_dev * choose * 9 // (experts * 8)
    slot_count = experts * capacity
    dispatch, counts = routing(expert_ids, experts, capacity)
    dispatch_pair = dispatch.astype(jnp.bfloat16)
    dispatch_tok = jnp.sum(dispatch.reshape(slot_count, tok_dev, choose), axis=2).astype(
        jnp.bfloat16
    )
    outgoing = jnp.dot(dispatch_tok, tokens, preferred_element_type=jnp.float32).astype(
        jnp.bfloat16
    )
    count_rows = jnp.zeros((experts, 1, features), jnp.bfloat16)
    count_rows = count_rows.at[:, 0, 0].set(counts.astype(jnp.bfloat16))
    payload = jnp.concatenate([outgoing.reshape(experts, capacity, features), count_rows], axis=1)
    arrived_all = lax.all_to_all(payload, "expert", split_axis=0, concat_axis=0, tiled=True)
    arrived = arrived_all[:, :capacity]
    arrived_counts = arrived_all[:, capacity, 0:1]
    upstream = cotangent.astype(jnp.float32)
    slot_probs = jnp.sum(jnp.where(dispatch, route_probs.reshape(1, tok_dev * choose), 0.0), axis=1)
    slot_cot = jnp.dot(dispatch_tok, cotangent, preferred_element_type=jnp.float32)
    outgoing_grad = (slot_probs[:, None] * slot_cot).astype(jnp.bfloat16)
    arrived_all, outgoing_grad = lax.optimization_barrier((arrived_all, outgoing_grad))
    arrived_grad = lax.all_to_all(
        outgoing_grad.reshape(experts, capacity, features),
        "expert",
        split_axis=0,
        concat_axis=0,
        tiled=True,
    )
    routed = arrived.reshape(slot_count, features)
    grad_rows = arrived_grad.reshape(slot_count, features)
    live_mask = jnp.arange(capacity, dtype=jnp.float32)[None, :] < arrived_counts.astype(
        jnp.float32
    )
    live_mask = live_mask.astype(jnp.float32).reshape(slot_count)
    w_gate = lax.all_gather(gate_weight, "fsdp", axis=1, tiled=True)[0]
    w_up = lax.all_gather(up_weight, "fsdp", axis=1, tiled=True)[0]
    w_down = lax.all_gather(down_weight, "fsdp", axis=2, tiled=True)[0]
    w_down_blocks = w_down.reshape(w_down.shape[0], n_fsdp, -1).swapaxes(0, 1)
    gate_pre, up_pre, hidden, expert_out = expert_forward(
        routed, live_mask, w_gate, w_up, w_down_blocks
    )
    returned = lax.all_to_all(
        expert_out.reshape(n_expert, capacity, features),
        "expert",
        split_axis=0,
        concat_axis=0,
        tiled=True,
    )
    row_grad, term_gate, term_up, term_down_t = expert_backward(
        routed, grad_rows, gate_pre, up_pre, hidden, w_gate, w_up, w_down_blocks
    )
    returned_grad = lax.all_to_all(
        row_grad.reshape(n_expert, capacity, features),
        "expert",
        split_axis=0,
        concat_axis=0,
        tiled=True,
    )
    summed_gate = lax.psum_scatter(
        term_gate.astype(jnp.bfloat16), "fsdp", scatter_dimension=0, tiled=True
    )
    returned, term_up = lax.optimization_barrier((returned, term_up))
    (summed_up,) = scatter_sum_fsdp([term_up], n_fsdp)
    summed_down = lax.psum_scatter(
        term_down_t.T.astype(jnp.bfloat16), "fsdp", scatter_dimension=1, tiled=True
    )
    combined = lax.dot_general(
        dispatch_pair,
        returned.reshape(slot_count, features),
        (((0,), (0,)), ((), ())),
        preferred_element_type=jnp.float32,
    ).reshape(tok_dev, choose, features)
    mixed = jnp.einsum("tk,tkd->td", route_probs, combined).astype(jnp.bfloat16)
    grad_probs = jnp.einsum("td,tkd->tk", upstream, combined)
    grad_tokens = lax.dot_general(
        dispatch_tok,
        returned_grad.reshape(slot_count, features),
        (((0,), (0,)), ((), ())),
        preferred_element_type=jnp.float32,
    ).astype(jnp.bfloat16)
    return (mixed, grad_probs, grad_tokens, summed_gate[None], summed_up[None], summed_down[None])


def solution(mesh):
    return jax.shard_map(
        per_device,
        mesh=mesh,
        in_specs=(
            P(("expert", "fsdp"), None),
            P(("expert", "fsdp"), None),
            P(("expert", "fsdp"), None),
            P("expert", "fsdp", None),
            P("expert", "fsdp", None),
            P("expert", None, "fsdp"),
            P(("expert", "fsdp"), None),
        ),
        out_specs=(
            P(("expert", "fsdp"), None),
            P(("expert", "fsdp"), None),
            P(("expert", "fsdp"), None),
            P("expert", "fsdp", None),
            P("expert", "fsdp", None),
            P("expert", None, "fsdp"),
        ),
        check_vma=False,
    )
```

profile of v0, /device:TPU:2, one launch (start us, length us, event | category | flops | bytes accessed | tf_op | source)
XLA Modules:
  0.0 421.8 jit_solution(11539978942677578161)
XLA Ops:
  7.2 0.7 all-gather.8.cloned.1.call-update
  8.0 0.7 all-gather.4.cloned.1.call-update
  8.7 0.8 copy.62
  9.7 1.2 reduce-window.6
  10.8 0.2 slice_reduce_fusion
  11.1 0.2 fusion.32
  11.5 0.7 multiply_add_fusion
  12.4 3.4 convolution_convert_fusion.2
  15.7 2.6 reshape.166
  18.3 2.0 fusion.16
  20.3 8.7 %all-to-all-start = ((bf16[16,37,2048]{2,1,0:T(8,128)(2,1)}), bf16[16,37,2048]{2,1,0:T(8,128)(2,1)S(1)}, u32[]{:S(2)}, u32[]{:S(2)}) async-start(bf16[16,37,2048]{2,1,0:T(8,128)(2,1)} %fusion.16), calls=%async_computation | async-start | bytes 5242880 | tf_op jit(solution)/shard_map/all_to_all | solution.py:81
  29.1 0.7 all-gather.6.cloned.1.call-update
  30.0 0.2 select_reduce_fusion
  30.2 2.2 multiply_convert_fusion
  32.5 57.1 %all-to-all-done = bf16[16,37,2048]{2,1,0:T(8,128)(2,1)S(1)} async-done(((bf16[16,37,2048]{2,1,0:T(8,128)(2,1)}), bf16[16,37,2048]{2,1,0:T(8,128)(2,1)S(1)}, u32[]{:S(2)}, u32[]{:S(2)}) %all-to-all-start) | async-done | bytes 2424864 | tf_op jit(solution)/shard_map/all_to_all | solution.py:81
  89.6 4.5 %reshape.168 = bf16[16,36,2048]{2,1,0:T(8,128)(2,1)} reshape(bf16[576,2048]{1,0:T(8,128)(2,1)} %multiply_convert_fusion) | data formatting | bytes 4718592 | tf_op jit(solution)/shard_map/reshape | solution.py:90
  94.1 4.6 %all-to-all-start.2 = ((bf16[16,36,2048]{2,1,0:T(8,128)(2,1)}), bf16[16,36,2048]{2,1,0:T(8,128)(2,1)S(1)}, u32[]{:S(2)}, u32[]{:S(2)}) async-start(bf16[16,36,2048]{2,1,0:T(8,128)(2,1)} %reshape.168), calls=%async_computation.2 | async-start | bytes 5242880 | tf_op jit(solution)/shard_map/all_to_all | solution.py:89
  98.7 1.0 fusion.34
  99.8 4.1 reshape.167
  103.9 4.4 %copy.83 = bf16[88,8,16,128]{3,2,1,0:T(8,128)(2,1)} copy(bf16[88,8,16,128]{3,1,2,0:T(8,128)(2,1)} %bitcast.86) | data formatting | bytes 5767168
  108.4 17.8 %all-gather.4.cloned.1.call-done = bf16[1,2048,704]{1,2,0:T(8,128)(2,1)} async-done(((bf16[1,128,704]{1,2,0:T(8,128)(2,1)}), bf16[1,2048,704]{1,2,0:T(8,128)(2,1)}) %all-gather.4.cloned.1.call-update) | async-done | bytes 2883600 | tf_op jit(solution)/shard_map/all_gather | solution.py:102
  126.1 5.8 %fusion.14 = f32[576,704]{1,0:T(8,128)} fusion(bf16[576,2048]{1,0:T(8,128)(2,1)} %reshape.167, bf16[1,2048,704]{1,2,0:T(8,128)(2,1)} %all-gather.4.cloned.1.call-done), kind=kOutput, calls=%fused_computation.20 | convolution fusion | flops 1660944384 | bytes 6864896 | tf_op jit(solution)/shard_map/dot_general | solution.py:19
  131.9 27.3 %all-to-all-done.2 = bf16[16,36,2048]{2,1,0:T(8,128)(2,1)S(1)} async-done(((bf16[16,36,2048]{2,1,0:T(8,128)(2,1)}), bf16[16,36,2048]{2,1,0:T(8,128)(2,1)S(1)}, u32[]{:S(2)}, u32[]{:S(2)}) %all-to-all-start.2) | async-done | bytes 2359328 | tf_op jit(solution)/shard_map/all_to_all | solution.py:89
  159.2 2.7 reshape_reshape.7
  161.9 5.8 %fusion.5 = f32[576,704,1]{1,0,2:T(8,128)} fusion(bf16[704,16,128]{2,1,0:T(8,128)(2,1)} %bitcast.87, bf16[576,16,128]{2,1,0:T(8,128)(2,1)} %reshape_reshape.7), kind=kOutput, calls=%fused_computation.11 | convolution fusion | flops 1660944384 | bytes 6864896 | tf_op jit(solution)/shard_map/sjd,jfd->sf/dot_general | solution.py:30
  167.7 15.9 %all-gather.6.cloned.1.call-done = bf16[1,2048,704]{1,2,0:T(8,128)(2,1)} async-done(((bf16[1,128,704]{1,2,0:T(8,128)(2,1)}), bf16[1,2048,704]{1,2,0:T(8,128)(2,1)}) %all-gather.6.cloned.1.call-update) | async-done | bytes 2883600 | tf_op jit(solution)/shard_map/all_gather | solution.py:103
  183.6 7.6 %fusion.25 = (bf16[576,704]{1,0:T(8,128)(2,1)}, bf16[576,704]{1,0:T(8,128)(2,1)}, bf16[576,704]{1,0:T(8,128)(2,1)S(1)}) fusion(f32[576,704,1]{1,0,2:T(8,128)} %fusion.5, f32[576,704]{1,0:T(8,128)} %fusion.14, f32[576]{0:T(1024)S(1)} %reshape.174, bf16[576,2048]{1,0:T(8,128)(2,1)} %reshape.167, bf16[1,2048,704]{1,2,0:T(8,128)(2,1)} %all-gather.6.cloned.1.call-done), kind=kOutput, calls=%fused_computation.33 | convolution fusion | flops 1667432448 | bytes 10922240 | tf_op jit(solution)/shard_map/dot_general | solution.py:20
  191.1 2.0 fusion.20
  193.2 2.9 copy.68
  196.1 4.5 %reshape_reshape.6 = bf16[16,36,2048]{2,1,0:T(8,128)(2,1)} reshape(bf16[576,16,128]{2,1,0:T(8,128)(2,1)} %copy.68) | data formatting | bytes 4718592 | tf_op jit(solution)/shard_map/reshape;reshape | solution.py:110
  200.6 7.2 %all-to-all-start.1 = ((bf16[16,36,2048]{2,1,0:T(8,128)(2,1)}), bf16[16,36,2048]{2,1,0:T(8,128)(2,1)}, u32[]{:S(2)}, u32[]{:S(2)}) async-start(bf16[16,36,2048]{2,1,0:T(8,128)(2,1)} %reshape_reshape.6), calls=%async_computation.1 | async-start | bytes 5242880 | tf_op jit(solution)/shard_map/all_to_all | solution.py:109
  207.8 0.3 reduce-scatter.9.cloned.1.call-start
  208.0 2.1 reshape.172
  210.2 4.4 %convolution_convert_fusion = bf16[704,2048]{1,0:T(8,128)(2,1)S(1)} fusion(bf16[576,704]{1,0:T(8,128)(2,1)} %copy-done.9, bf16[576,2048]{1,0:T(8,128)(2,1)} %reshape.172), kind=kOutput, calls=%fused_computation.8 | convolution fusion | flops 1662386176 | bytes 6053888 | tf_op jit(solution)/shard_map/dot_general | solution.py:44
  214.5 2.8 copy.80
  217.4 1.8 copy-done.6
  219.2 3.3 fusion.12
  222.5 2.0 add_convert_fusion
  224.5 2.2 reshape.170
  226.7 41.6 %all-to-all-done.1 = bf16[16,36,2048]{2,1,0:T(8,128)(2,1)} async-done(((bf16[16,36,2048]{2,1,0:T(8,128)(2,1)}), bf16[16,36,2048]{2,1,0:T(8,128)(2,1)}, u32[]{:S(2)}, u32[]{:S(2)}) %all-to-all-start.1) | async-done | bytes 2359328 | tf_op jit(solution)/shard_map/all_to_all | solution.py:109
  268.4 4.6 %all-to-all-start.3 = ((bf16[16,36,2048]{2,1,0:T(8,128)(2,1)}), bf16[16,36,2048]{2,1,0:T(8,128)(2,1)S(1)}, u32[]{:S(2)}, u32[]{:S(2)}) async-start(bf16[16,36,2048]{2,1,0:T(8,128)(2,1)} %reshape.170), calls=%async_computation.3 | async-start | bytes 5242880 | tf_op jit(solution)/shard_map/all_to_all | solution.py:119
  273.0 5.9 %convolution_convert_fusion.1 = bf16[2048,704]{0,1:T(8,128)(2,1)} fusion(bf16[576,2048]{1,0:T(8,128)(2,1)} %reshape.167, bf16[576,704]{1,0:T(8,128)(2,1)} %get-tuple-element.26), kind=kOutput, calls=%fused_computation.9 | convolution fusion | flops 1662386176 | bytes 6053888 | tf_op jit(solution)/shard_map/dot_general | solution.py:42
  279.0 4.6 %copy.78 = bf16[2048,704]{1,0:T(8,128)(2,1)} copy(bf16[2048,704]{0,1:T(8,128)(2,1)} %convolution_convert_fusion.1) | data formatting | bytes 5767168
  283.6 4.3 %fusion.39 = bf16[2048,704]{0,1:T(8,128)(2,1)S(1)} fusion(bf16[576,2048]{1,0:T(8,128)(2,1)} %reshape.167, bf16[576,704]{1,0:T(8,128)(2,1)} %get-tuple-element.27), kind=kOutput, calls=%fused_computation.67 | convolution fusion | flops 1660944384 | bytes 6053888 | tf_op jit(solution)/shard_map/dot_general | solution.py:43
  287.9 0.9 copy.84
  288.9 2.3 copy.72
  291.2 42.3 %all-to-all-done.3 = bf16[16,36,2048]{2,1,0:T(8,128)(2,1)S(1)} async-done(((bf16[16,36,2048]{2,1,0:T(8,128)(2,1)}), bf16[16,36,2048]{2,1,0:T(8,128)(2,1)S(1)}, u32[]{:S(2)}, u32[]{:S(2)}) %all-to-all-start.3) | async-done | bytes 2359328 | tf_op jit(solution)/shard_map/all_to_all | solution.py:119
  333.5 1.5 copy-done.2
  335.0 5.7 %all-to-all-start.4 = ((bf16[16,1,128,704]{2,3,1,0:T(8,128)(2,1)}), bf16[16,1,128,704]{2,3,1,0:T(8,128)(2,1)S(1)}, u32[]{:S(2)}, u32[]{:S(2)}) async-start(bf16[16,1,128,704]{2,3,1,0:T(8,128)(2,1)} %copy.72), calls=%async_computation.4 | async-start | bytes 5767168 | tf_op jit(solution)/shard_map/all_to_all | solution.py:57
  340.7 0.2 copy.74
  340.9 1.0 iota_compare_fusion.1
  341.9 2.1 eq.68
  344.0 4.1 reshape.177
  348.1 3.6 fusion.27
  351.7 1.7 fusion.3
  353.5 1.1 copy.107
  354.5 2.8 fusion.1
  357.3 0.7 copy.77
  358.0 4.1 reshape.171
  362.1 3.2 convolution_convert_fusion.3
  365.3 1.7 copy.81
  367.1 45.4 %reduce-scatter.7.cloned.1.call-done = bf16[128,704]{1,0:T(8,128)(2,1)} async-done(((bf16[2048,704]{1,0:T(8,128)(2,1)}), bf16[128,704]{1,0:T(8,128)(2,1)}) %reduce-scatter.7.cloned.1.call-update) | async-done | bytes 180240
  412.4 1.7 copy.79
  414.2 1.1 reduce_sum.57
  (42 shorter events, 1.3 us)
Async XLA Ops:
  7.2 23.1 %copy-start = (bf16[128,2048]{1,0:T(8,128)(2,1)S(1)}, bf16[128,2048]{1,0:T(8,128)(2,1)}, u32[]{:S(2)}) copy-start(bf16[128,2048]{1,0:T(8,128)(2,1)} %param.15) | copy-start | bytes 1572868
  7.2 96.8 %all-gather.8.cloned.1.call-start = ((), (), s32[]{:S(2)}) async-start(), calls=%async_computation.9 | async-start | bytes 3063808 | tf_op jit(solution)/shard_map/all_gather | solution.py:104
  7.9 118.2 %all-gather.4.cloned.1.call-start = ((), (), s32[]{:S(2)}) async-start(), calls=%async_computation.7 | async-start | bytes 3063808 | tf_op jit(solution)/shard_map/all_gather | solution.py:102
  12.4 17.8 %copy-start.3 = (s32[576,128]{1,0:T(8,128)}, s32[576,128]{1,0:T(8,128)S(1)}, u32[]{:S(2)}) copy-start(s32[576,128]{1,0:T(8,128)S(1)} %convert_reduce_fusion) | copy-start | bytes 884740
  20.3 9.5 %copy-start.5 = (f32[128,4]{0,1:T(4,128)S(1)}, f32[128,4]{0,1:T(4,128)}, u32[]{:S(2)}) copy-start(f32[128,4]{0,1:T(4,128)} %param.11) | copy-start | bytes 6148
  20.3 69.2 %all-to-all-start = ((bf16[16,37,2048]{2,1,0:T(8,128)(2,1)}), bf16[16,37,2048]{2,1,0:T(8,128)(2,1)S(1)}, u32[]{:S(2)}, u32[]{:S(2)}) async-start(bf16[16,37,2048]{2,1,0:T(8,128)(2,1)} %fusion.16), calls=%async_computation | async-start | bytes 5242880 | tf_op jit(solution)/shard_map/all_to_all | solution.py:81
  29.0 154.6 %all-gather.6.cloned.1.call-start = ((), (), s32[]{:S(2)}) async-start(), calls=%async_computation.8 | async-start | bytes 3063808 | tf_op jit(solution)/shard_map/all_gather | solution.py:103
  89.6 4.5 %copy-start.1 = (bf16[16,37,2048]{2,1,0:T(8,128)(2,1)}, bf16[16,37,2048]{2,1,0:T(8,128)(2,1)S(1)}, u32[]{:S(2)}) copy-start(bf16[16,37,2048]{2,1,0:T(8,128)(2,1)S(1)} %all-to-all-done) | copy-start | bytes 7274500
  94.1 65.1 %all-to-all-start.2 = ((bf16[16,36,2048]{2,1,0:T(8,128)(2,1)}), bf16[16,36,2048]{2,1,0:T(8,128)(2,1)S(1)}, u32[]{:S(2)}, u32[]{:S(2)}) async-start(bf16[16,36,2048]{2,1,0:T(8,128)(2,1)} %reshape.168), calls=%async_computation.2 | async-start | bytes 5242880 | tf_op jit(solution)/shard_map/all_to_all | solution.py:89
  183.6 7.6 %copy-start.4 = (bf16[88,8,16,128]{3,2,1,0:T(8,128)(2,1)S(1)}, bf16[88,8,16,128]{3,2,1,0:T(8,128)(2,1)}, u32[]{:S(2)}) copy-start(bf16[88,8,16,128]{3,2,1,0:T(8,128)(2,1)} %copy.83) | copy-start | bytes 8650756
  191.1 2.0 copy-start.9
  200.6 67.8 %all-to-all-start.1 = ((bf16[16,36,2048]{2,1,0:T(8,128)(2,1)}), bf16[16,36,2048]{2,1,0:T(8,128)(2,1)}, u32[]{:S(2)}, u32[]{:S(2)}) async-start(bf16[16,36,2048]{2,1,0:T(8,128)(2,1)} %reshape_reshape.6), calls=%async_computation.1 | async-start | bytes 5242880 | tf_op jit(solution)/shard_map/all_to_all | solution.py:109
  207.8 157.6 %reduce-scatter.9.cloned.1.call-start = ((), (), s32[]{:S(2)}) async-start(), calls=%async_computation.11 | async-start | bytes 3342336
  217.3 1.8 copy-start.6
  219.2 3.3 copy-start.7
  219.2 3.3 copy-start.8
  268.4 65.1 %all-to-all-start.3 = ((bf16[16,36,2048]{2,1,0:T(8,128)(2,1)}), bf16[16,36,2048]{2,1,0:T(8,128)(2,1)S(1)}, u32[]{:S(2)}, u32[]{:S(2)}) async-start(bf16[16,36,2048]{2,1,0:T(8,128)(2,1)} %reshape.170), calls=%async_computation.3 | async-start | bytes 5242880 | tf_op jit(solution)/shard_map/all_to_all | solution.py:119
  273.0 139.5 %reduce-scatter.7.cloned.1.call-start = ((), (), s32[]{:S(2)}) async-start(), calls=%async_computation.10 | async-start | bytes 3342336
  333.5 1.5 copy-start.2
  335.0 79.2 %all-to-all-start.4 = ((bf16[16,1,128,704]{2,3,1,0:T(8,128)(2,1)}), bf16[16,1,128,704]{2,3,1,0:T(8,128)(2,1)S(1)}, u32[]{:S(2)}, u32[]{:S(2)}) async-start(bf16[16,1,128,704]{2,3,1,0:T(8,128)(2,1)} %copy.72), calls=%async_computation.4 | async-start | bytes 5767168 | tf_op jit(solution)/shard_map/all_to_all | solution.py:57
Sparse Core Ops, SparseCore 0:
  10.4 58.2 all-gather.7
  71.1 55.0 all-gather.3
  128.5 55.0 all-gather.5
  217.5 81.1 reduce-scatter.8
  302.1 110.2 reduce-scatter.6
where the time goes:
time: 423 us; the launch traced here: 422 us
  waiting for transfers between devices  250 us (59%)
  local copies, waits for them, and re-layouts  61.6 us (15%)
  matrix products  58 us (14%)
  starting transfers between devices  31.2 us (7%)
  between operations  14 us (3%)
  other arithmetic  7.5 us (2%)
    all_to_all x1, waiting for transfers between devices, per_device(): lax.all_to_all(payload, 'expert', split_axis=0, concat_axis=0, tiled=True)  57.1 us
    unnamed x7, waiting for transfers between devices  47.5 us
    all_to_all x1, waiting for transfers between devices, per_device(): lax.all_to_all(row_grad.reshape(n_expert, capacity, features), 'expert',...  42.3 us
    all_to_all x1, waiting for transfers between devices, per_device(): lax.all_to_all(expert_out.reshape(n_expert, capacity, features), 'expert'...  41.6 us
    all_to_all x1, waiting for transfers between devices, per_device(): lax.all_to_all(outgoing_grad.reshape(experts, capacity, features), 'exper...  27.3 us
    unnamed x29, local copies, waits for them, and re-layouts  20.6 us
    all_gather x1, waiting for transfers between devices, per_device(): w_gate = lax.all_gather(gate_weight, 'fsdp', axis=1, tiled=True)[0]  17.8 us
    all_gather x1, waiting for transfers between devices, per_device(): w_up = lax.all_gather(up_weight, 'fsdp', axis=1, tiled=True)[0]  15.9 us
  transfers between devices with their start and end apart: 10, of which 7 were waited for; matrix products, arithmetic and copies ran while one was open for 25% of the time, Pallas kernels for 0%

commit v1 on v0

--- a/solution.py
+++ b/solution.py
@@ -99,7 +99,9 @@
         jnp.float32
     )
     live_mask = live_mask.astype(jnp.float32).reshape(slot_count)
-    w_gate = lax.all_gather(gate_weight, "fsdp", axis=1, tiled=True)[0]
+    w_gate = jnp.concatenate(
+        lax.all_to_all(jnp.stack([gate_weight] * lax.axis_size("fsdp")), "fsdp", 0, 0), axis=1
+    )[0]
     w_up = lax.all_gather(up_weight, "fsdp", axis=1, tiled=True)[0]
     w_down = lax.all_gather(down_weight, "fsdp", axis=2, tiled=True)[0]
     w_down_blocks = w_down.reshape(w_down.shape[0], n_fsdp, -1).swapaxes(0, 1)

time: 423 us -> 462 us (1.092); the launches traced: 422 us -> 454 us
  waiting for transfers between devices: 250 us -> 261 us
  local copies, waits for them, and re-layouts: 61.6 us -> 71.9 us
  starting transfers between devices: 31.2 us -> 40.3 us
    all_to_all x0 -> x1, waiting for transfers between devices: none -> 30.6 us  [per_device(): lax.all_to_all(jnp.stack([gate_weight] * lax.axis_size('fsdp')), 'fsdp',...]
    all_gather x1 -> x0, waiting for transfers between devices: 17.8 us -> none  [per_device(): w_gate = lax.all_gather(gate_weight, 'fsdp', axis=1, tiled=True)[0]]
    all_gather x1, waiting for transfers between devices: 15.9 us -> 0.01 us  [per_device(): w_up = lax.all_gather(up_weight, 'fsdp', axis=1, tiled=True)[0]]
    all_to_all x1, waiting for transfers between devices: 27.3 us -> 39.7 us  [per_device(): lax.all_to_all(outgoing_grad.reshape(experts, capacity, features), 'exper...]
    all_to_all x0 -> x1, starting transfers between devices: none -> 7.61 us  [per_device(): lax.all_to_all(jnp.stack([gate_weight] * lax.axis_size('fsdp')), 'fsdp',...]
    all_to_all x0 -> x1, local copies, waits for them, and re-layouts: none -> 5.27 us  [per_device(): lax.all_to_all(jnp.stack([gate_weight] * lax.axis_size('fsdp')), 'fsdp',...]
    unnamed x29 -> x33, local copies, waits for them, and re-layouts: 20.6 us -> 23.2 us
    unnamed x7 -> x6, waiting for transfers between devices: 47.5 us -> 47.6 us
  transfers between devices with their start and end apart: 10 -> 10, of which waited for: 7 -> 6; matrix products, arithmetic and copies ran while one was open for 25% -> 23% of each run, Pallas kernels for 0% -> 0%
where the time goes in v1:
time: 462 us; the launch traced here: 454 us
  waiting for transfers between devices  261 us (56%)
  local copies, waits for them, and re-layouts  71.9 us (16%)
  matrix products  58.9 us (13%)
  starting transfers between devices  40.3 us (9%)
  between operations  14.2 us (3%)
  other arithmetic  7.38 us (2%)
    all_to_all x1, waiting for transfers between devices, per_device(): lax.all_to_all(payload, 'expert', split_axis=0, concat_axis=0, tiled=True)  59.8 us
    unnamed x6, waiting for transfers between devices  47.6 us
    all_to_all x1, waiting for transfers between devices, per_device(): lax.all_to_all(row_grad.reshape(n_expert, capacity, features), 'expert',...  42.1 us
    all_to_all x1, waiting for transfers between devices, per_device(): lax.all_to_all(expert_out.reshape(n_expert, capacity, features), 'expert'...  41.7 us
    all_to_all x1, waiting for transfers between devices, per_device(): lax.all_to_all(outgoing_grad.reshape(experts, capacity, features), 'exper...  39.7 us
    all_to_all x1, waiting for transfers between devices, per_device(): lax.all_to_all(jnp.stack([gate_weight] * lax.axis_size('fsdp')), 'fsdp',...  30.6 us
    unnamed x33, local copies, waits for them, and re-layouts  23.2 us
  transfers between devices with their start and end apart: 10, of which 6 were waited for; matrix products, arithmetic and copies ran while one was open for 23% of the time, Pallas kernels for 0%

profile of v1, /device:TPU:2, one launch (start us, length us, event | category | flops | bytes accessed | tf_op | source)
XLA Modules:
  0.0 454.2 jit_solution(8451166815954876035)
XLA Ops:
  7.2 0.8 copy.79
  8.3 1.2 reduce-window.6
  9.4 0.2 slice_reduce_fusion
  10.1 0.7 multiply_add_fusion
  11.0 0.7 copy-done.4
  11.7 3.2 convolution_convert_fusion.2
  14.9 2.6 reshape.169
  17.5 1.8 fusion.16
  19.4 8.7 %all-to-all-start = ((bf16[16,37,2048]{2,1,0:T(8,128)(2,1)}), bf16[16,37,2048]{2,1,0:T(8,128)(2,1)S(1)}, u32[]{:S(2)}, u32[]{:S(2)}) async-start(bf16[16,37,2048]{2,1,0:T(8,128)(2,1)} %fusion.16), calls=%async_computation | async-start | bytes 5242880 | tf_op jit(solution)/shard_map/all_to_all | solution.py:81
  28.1 0.7 all-gather.5.cloned.1.call-update
  28.8 59.8 %all-to-all-done = bf16[16,37,2048]{2,1,0:T(8,128)(2,1)S(1)} async-done(((bf16[16,37,2048]{2,1,0:T(8,128)(2,1)}), bf16[16,37,2048]{2,1,0:T(8,128)(2,1)S(1)}, u32[]{:S(2)}, u32[]{:S(2)}) %all-to-all-start) | async-done | bytes 2424864 | tf_op jit(solution)/shard_map/all_to_all | solution.py:81
  88.6 2.4 stack.2
  91.0 7.6 %all-to-all-start.1 = ((bf16[16,1,128,704]{2,3,1,0:T(8,128)(2,1)}), bf16[16,1,128,704]{2,3,1,0:T(8,128)(2,1)S(1)}, u32[]{:S(2)}, u32[]{:S(2)}) async-start(bf16[16,1,128,704]{2,3,1,0:T(8,128)(2,1)} %stack.2), calls=%async_computation.1 | async-start | bytes 5767168 | tf_op jit(solution)/shard_map/all_to_all | solution.py:103
  98.6 0.7 all-gather.3.cloned.1.call-update
  99.6 0.2 select_reduce_fusion
  99.8 3.2 multiply_convert_fusion
  103.0 4.1 reshape.171
  107.0 30.6 %all-to-all-done.1 = bf16[16,1,128,704]{2,3,1,0:T(8,128)(2,1)S(1)} async-done(((bf16[16,1,128,704]{2,3,1,0:T(8,128)(2,1)}), bf16[16,1,128,704]{2,3,1,0:T(8,128)(2,1)S(1)}, u32[]{:S(2)}, u32[]{:S(2)}) %all-to-all-start.1) | async-done | bytes 2883616 | tf_op jit(solution)/shard_map/all_to_all | solution.py:103
  137.6 1.6 copy-done.1
  139.2 6.9 %all-to-all-start.3 = ((bf16[16,36,2048]{2,1,0:T(8,128)(2,1)}), bf16[16,36,2048]{2,1,0:T(8,128)(2,1)S(1)}, u32[]{:S(2)}, u32[]{:S(2)}) async-start(bf16[16,36,2048]{2,1,0:T(8,128)(2,1)} %reshape.171), calls=%async_computation.3 | async-start | bytes 5242880 | tf_op jit(solution)/shard_map/all_to_all | solution.py:89
  146.1 5.3 %copy.84 = bf16[16,1,128,704]{2,0,3,1:T(8,128)(2,1)} copy(bf16[16,1,128,704]{2,3,1,0:T(8,128)(2,1)} %copy-done.1) | data formatting | bytes 5767168 | tf_op jit(solution)/shard_map/all_to_all | solution.py:103
  151.3 1.0 fusion.36
  152.5 4.1 reshape.170
  156.6 5.9 %fusion.7 = f32[576,704]{1,0:T(8,128)} fusion(bf16[576,2048]{1,0:T(8,128)(2,1)} %reshape.170, bf16[88,8,16,128]{3,2,1,0:T(8,128)(2,1)} %bitcast.91), kind=kOutput, calls=%fused_computation.13 | convolution fusion | flops 1660944384 | bytes 6864896 | tf_op jit(solution)/shard_map/dot_general | solution.py:19
  162.5 4.4 copy.102
  166.9 39.7 %all-to-all-done.3 = bf16[16,36,2048]{2,1,0:T(8,128)(2,1)S(1)} async-done(((bf16[16,36,2048]{2,1,0:T(8,128)(2,1)}), bf16[16,36,2048]{2,1,0:T(8,128)(2,1)S(1)}, u32[]{:S(2)}, u32[]{:S(2)}) %all-to-all-start.3) | async-done | bytes 2359328 | tf_op jit(solution)/shard_map/all_to_all | solution.py:89
  206.6 3.1 reshape_reshape.7
  209.7 5.8 %fusion.9 = f32[576,704,1]{1,0,2:T(8,128)} fusion(bf16[704,16,128]{2,1,0:T(8,128)(2,1)} %bitcast.94, bf16[576,16,128]{2,1,0:T(8,128)(2,1)} %reshape_reshape.7), kind=kOutput, calls=%fused_computation.15 | convolution fusion | flops 1660944384 | bytes 6864896 | tf_op jit(solution)/shard_map/sjd,jfd->sf/dot_general | solution.py:30
  215.5 7.6 %fusion.27 = (bf16[576,704]{1,0:T(8,128)(2,1)}, bf16[576,704]{1,0:T(8,128)(2,1)}, bf16[576,704]{1,0:T(8,128)(2,1)S(1)}) fusion(f32[576,704,1]{1,0,2:T(8,128)} %fusion.9, f32[576,704]{1,0:T(8,128)} %fusion.7, f32[576]{0:T(1024)S(1)} %reshape.177, bf16[576,2048]{1,0:T(8,128)(2,1)} %reshape.170, bf16[1,2048,704]{1,2,0:T(8,128)(2,1)} %all-gather.3.cloned.1.call-done), kind=kOutput, calls=%fused_computation.35 | convolution fusion | flops 1667432448 | bytes 10922240 | tf_op jit(solution)/shard_map/dot_general | solution.py:20
  223.1 2.0 fusion.22
  225.1 2.9 copy.86
  228.0 4.5 reshape_reshape.6
  232.5 4.6 %all-to-all-start.2 = ((bf16[16,36,2048]{2,1,0:T(8,128)(2,1)}), bf16[16,36,2048]{2,1,0:T(8,128)(2,1)}, u32[]{:S(2)}, u32[]{:S(2)}) async-start(bf16[16,36,2048]{2,1,0:T(8,128)(2,1)} %reshape_reshape.6), calls=%async_computation.2 | async-start | bytes 5242880 | tf_op jit(solution)/shard_map/all_to_all | solution.py:111
  237.2 2.3 reshape.175
  239.5 4.4 convolution_convert_fusion
  243.9 2.8 copy.98
  246.7 1.8 copy-done.5
  248.5 3.3 fusion.5
  251.9 2.0 add_convert_fusion
  253.9 2.2 reshape.173
  256.1 41.7 %all-to-all-done.2 = bf16[16,36,2048]{2,1,0:T(8,128)(2,1)} async-done(((bf16[16,36,2048]{2,1,0:T(8,128)(2,1)}), bf16[16,36,2048]{2,1,0:T(8,128)(2,1)}, u32[]{:S(2)}, u32[]{:S(2)}) %all-to-all-start.2) | async-done | bytes 2359328 | tf_op jit(solution)/shard_map/all_to_all | solution.py:111
  297.8 4.6 %all-to-all-start.4 = ((bf16[16,36,2048]{2,1,0:T(8,128)(2,1)}), bf16[16,36,2048]{2,1,0:T(8,128)(2,1)S(1)}, u32[]{:S(2)}, u32[]{:S(2)}) async-start(bf16[16,36,2048]{2,1,0:T(8,128)(2,1)} %reshape.173), calls=%async_computation.4 | async-start | bytes 5242880 | tf_op jit(solution)/shard_map/all_to_all | solution.py:121
  302.4 5.9 %convolution_convert_fusion.1 = bf16[2048,704]{0,1:T(8,128)(2,1)} fusion(bf16[576,2048]{1,0:T(8,128)(2,1)} %reshape.170, bf16[576,704]{1,0:T(8,128)(2,1)} %get-tuple-element.26), kind=kOutput, calls=%fused_computation.9 | convolution fusion | flops 1662386176 | bytes 6053888 | tf_op jit(solution)/shard_map/dot_general | solution.py:42
  308.3 4.8 %copy.96 = bf16[2048,704]{1,0:T(8,128)(2,1)} copy(bf16[2048,704]{0,1:T(8,128)(2,1)} %convolution_convert_fusion.1) | data formatting | bytes 5767168
  313.2 4.4 fusion.41
  317.5 0.9 copy.103
  318.5 2.3 copy.90
  320.8 42.1 %all-to-all-done.4 = bf16[16,36,2048]{2,1,0:T(8,128)(2,1)S(1)} async-done(((bf16[16,36,2048]{2,1,0:T(8,128)(2,1)}), bf16[16,36,2048]{2,1,0:T(8,128)(2,1)S(1)}, u32[]{:S(2)}, u32[]{:S(2)}) %all-to-all-start.4) | async-done | bytes 2359328 | tf_op jit(solution)/shard_map/all_to_all | solution.py:121
  362.9 1.5 copy-done.3
  364.4 7.7 %all-to-all-start.5 = ((bf16[16,1,128,704]{2,3,1,0:T(8,128)(2,1)}), bf16[16,1,128,704]{2,3,1,0:T(8,128)(2,1)S(1)}, u32[]{:S(2)}, u32[]{:S(2)}) async-start(bf16[16,1,128,704]{2,3,1,0:T(8,128)(2,1)} %copy.90), calls=%async_computation.5 | async-start | bytes 5767168 | tf_op jit(solution)/shard_map/all_to_all | solution.py:57
  372.3 1.0 iota_compare_fusion.1
  373.2 2.1 eq.68
  375.4 4.2 reshape.180
  379.5 3.6 fusion.29
  383.1 1.7 fusion.3
  384.8 1.1 copy.134
  385.9 2.8 fusion.1
  388.7 0.7 copy.95
  389.4 4.1 reshape.174
  393.5 3.2 convolution_convert_fusion.3
  396.7 1.7 copy.99
  398.5 46.2 %reduce-scatter.7.cloned.1.call-done = bf16[128,704]{1,0:T(8,128)(2,1)} async-done(((bf16[2048,704]{1,0:T(8,128)(2,1)}), bf16[128,704]{1,0:T(8,128)(2,1)}) %reduce-scatter.7.cloned.1.call-update) | async-done | bytes 180240
  444.6 1.7 copy.97
  446.4 1.1 reduce_sum.57
  (47 shorter events, 1.6 us)
Async XLA Ops:
  7.2 92.6 %copy-start = (bf16[128,2048]{1,0:T(8,128)(2,1)S(1)}, bf16[128,2048]{1,0:T(8,128)(2,1)}, u32[]{:S(2)}) copy-start(bf16[128,2048]{1,0:T(8,128)(2,1)} %param.15) | copy-start | bytes 1572868
  10.9 0.7 copy-start.4
  19.4 69.2 %copy-start.7 = (bf16[1,128,704]{1,2,0:T(8,128)(2,1)S(1)}, bf16[1,128,704]{1,2,0:T(8,128)(2,1)}, u32[]{:S(2)}) copy-start(bf16[1,128,704]{1,2,0:T(8,128)(2,1)} %param.12) | copy-start | bytes 540676
  19.4 69.2 %all-to-all-start = ((bf16[16,37,2048]{2,1,0:T(8,128)(2,1)}), bf16[16,37,2048]{2,1,0:T(8,128)(2,1)S(1)}, u32[]{:S(2)}, u32[]{:S(2)}) async-start(bf16[16,37,2048]{2,1,0:T(8,128)(2,1)} %fusion.16), calls=%async_computation | async-start | bytes 5242880 | tf_op jit(solution)/shard_map/all_to_all | solution.py:81
  28.1 134.4 %all-gather.5.cloned.1.call-start = ((), (), s32[]{:S(2)}) async-start(), calls=%async_computation.9 | async-start | bytes 3063808 | tf_op jit(solution)/shard_map/all_gather | solution.py:106
  88.6 2.4 copy-start.2
  91.0 8.4 %copy-start.8 = (f32[128,4]{0,1:T(4,128)S(1)}, f32[128,4]{0,1:T(4,128)}, u32[]{:S(2)}) copy-start(f32[128,4]{0,1:T(4,128)} %param.11) | copy-start | bytes 6148
  91.0 46.7 %all-to-all-start.1 = ((bf16[16,1,128,704]{2,3,1,0:T(8,128)(2,1)}), bf16[16,1,128,704]{2,3,1,0:T(8,128)(2,1)S(1)}, u32[]{:S(2)}, u32[]{:S(2)}) async-start(bf16[16,1,128,704]{2,3,1,0:T(8,128)(2,1)} %stack.2), calls=%async_computation.1 | async-start | bytes 5767168 | tf_op jit(solution)/shard_map/all_to_all | solution.py:103
  98.6 116.9 %all-gather.3.cloned.1.call-start = ((), (), s32[]{:S(2)}) async-start(), calls=%async_computation.8 | async-start | bytes 3063808 | tf_op jit(solution)/shard_map/all_gather | solution.py:105
  137.6 1.6 copy-start.1
  139.2 67.4 %all-to-all-start.3 = ((bf16[16,36,2048]{2,1,0:T(8,128)(2,1)}), bf16[16,36,2048]{2,1,0:T(8,128)(2,1)S(1)}, u32[]{:S(2)}, u32[]{:S(2)}) async-start(bf16[16,36,2048]{2,1,0:T(8,128)(2,1)} %reshape.171), calls=%async_computation.3 | async-start | bytes 5242880 | tf_op jit(solution)/shard_map/all_to_all | solution.py:89
  215.5 7.6 %copy-start.6 = (bf16[88,8,16,128]{3,2,1,0:T(8,128)(2,1)S(1)}, bf16[88,8,16,128]{3,2,1,0:T(8,128)(2,1)}, u32[]{:S(2)}) copy-start(bf16[88,8,16,128]{3,2,1,0:T(8,128)(2,1)} %copy.102) | copy-start | bytes 8650756
  223.1 2.0 copy-start.11
  232.5 65.2 %all-to-all-start.2 = ((bf16[16,36,2048]{2,1,0:T(8,128)(2,1)}), bf16[16,36,2048]{2,1,0:T(8,128)(2,1)}, u32[]{:S(2)}, u32[]{:S(2)}) async-start(bf16[16,36,2048]{2,1,0:T(8,128)(2,1)} %reshape_reshape.6), calls=%async_computation.2 | async-start | bytes 5242880 | tf_op jit(solution)/shard_map/all_to_all | solution.py:111
  237.2 159.6 %reduce-scatter.9.cloned.1.call-start = ((), (), s32[]{:S(2)}) async-start(), calls=%async_computation.11 | async-start | bytes 3342336
  246.7 1.8 copy-start.5
  248.5 3.3 copy-start.9
  248.5 3.3 copy-start.10
  297.8 65.1 %all-to-all-start.4 = ((bf16[16,36,2048]{2,1,0:T(8,128)(2,1)}), bf16[16,36,2048]{2,1,0:T(8,128)(2,1)S(1)}, u32[]{:S(2)}, u32[]{:S(2)}) async-start(bf16[16,36,2048]{2,1,0:T(8,128)(2,1)} %reshape.173), calls=%async_computation.4 | async-start | bytes 5242880 | tf_op jit(solution)/shard_map/all_to_all | solution.py:121
  302.4 142.3 %reduce-scatter.7.cloned.1.call-start = ((), (), s32[]{:S(2)}) async-start(), calls=%async_computation.10 | async-start | bytes 3342336
  362.9 1.5 copy-start.3
  364.4 81.9 %all-to-all-start.5 = ((bf16[16,1,128,704]{2,3,1,0:T(8,128)(2,1)}), bf16[16,1,128,704]{2,3,1,0:T(8,128)(2,1)S(1)}, u32[]{:S(2)}, u32[]{:S(2)}) async-start(bf16[16,1,128,704]{2,3,1,0:T(8,128)(2,1)} %copy.90), calls=%async_computation.5 | async-start | bytes 5767168 | tf_op jit(solution)/shard_map/all_to_all | solution.py:57
Sparse Core Ops, SparseCore 0:
  31.3 56.8 all-gather.4
  101.8 67.9 all-gather.2
  246.9 83.0 reduce-scatter.8
  333.4 111.1 reduce-scatter.6
